TPU v7x, 512 devices: a whole 4x8x8 slice. The times are simulated.
512 devices in a mesh: wide: 32 (over z, x), tensor: 16 (over y, core).
Axes of the slice: x: 4, y: 8, z: 8, core: 2. Of those that a mesh axis runs over, the one named last changes fastest.
Arguments:
- tokens: bfloat16 [16384, 8192], P('wide', 'tensor'), may hold values from -6 to 6
- key_value_weight: bfloat16 [8192, 2048], P(None, 'tensor'), may hold values from -0.0625 to 0.0625
- adapter_down_maps: bfloat16 [8192, 512, 64], P('tensor', 'wide'), may hold values from -0.0625 to 0.0625
- adapter_up_maps: bfloat16 [512, 64, 2048], P('wide', None, 'tensor'), may hold values from -0.75 to 0.75
- adapter_per_row: int32 [16384], P('wide'), may hold values from 0 to 511, as said below
- adapter_storage_slot: int32 [512], replicated, may hold values from 0 to 511, as said below
Outputs:
- kv_out: bfloat16 [16384, 2048], P('wide', 'tensor')
Inputs may be any that keep to these rules, and one draw needn't show every extreme that they name: `adapter_per_row`: the adapter stored at position p belongs to owner p // 16 of wide. Among the 512 rows of one index of wide, at most 32 name adapters of one owner; in every draw one owner gets exactly 32 rows from every index of wide. `adapter_storage_slot`: each position is taken by exactly one adapter.
All inputs are finite; a program needn't handle non-finite values.
Results may differ from a plain program's by a relative error of at most 0.0049.
Values may be sent and summed in bfloat16 or wider, within the bound.
No kernel may reach another device: no remote copies, remote signals or barrier semaphores. Data moves between devices by JAX's collectives and lax.ppermute only.
A program may use at most 64 MiB of HBM per device.

v0:
```python
import jax
import jax.numpy as jnp
from jax import lax
from jax.sharding import PartitionSpec as P


def body(
    tokens,
    key_value_weight,
    adapter_down_maps,
    adapter_up_maps,
    adapter_per_row,
    adapter_storage_slot,
):
    row_count = tokens.shape[0]
    feature_portion = tokens.shape[1]
    wide_count = lax.axis_size("wide")
    capacity = 2 * row_count // wide_count
    present_adapters = adapter_down_maps.shape[1]
    rank_dimension = adapter_down_maps.shape[2]
    column_portion = key_value_weight.shape[1]
    gathered = lax.all_gather(tokens, "tensor", axis=1, tiled=True)
    base_projection_output = jnp.dot(gathered, key_value_weight, preferred_element_type=jnp.float32)
    total_adapters = adapter_storage_slot.shape[0]
    adapter_match = adapter_per_row[:, None] == jnp.arange(total_adapters, dtype=jnp.int32)[None, :]
    storage_position = jnp.sum(jnp.where(adapter_match, adapter_storage_slot[None, :], 0), axis=1)
    owner_index = storage_position // present_adapters
    local_index = storage_position % present_adapters
    owner_onehot = (
        owner_index[:, None] == jnp.arange(wide_count, dtype=jnp.int32)[None, :]
    ).astype(jnp.int32)
    earlier = jnp.cumsum(owner_onehot, axis=0) - owner_onehot
    rank_in_owner = jnp.sum(earlier * owner_onehot, axis=1)
    storage_slot_index = owner_index * capacity + rank_in_owner
    send_rows = (
        jnp.zeros((wide_count * capacity, feature_portion), jnp.bfloat16)
        .at[storage_slot_index]
        .set(tokens)
    )
    send_slots = (
        jnp.full((wide_count * capacity,), -1, jnp.int32).at[storage_slot_index].set(local_index)
    )
    send_rows = send_rows.reshape(wide_count, capacity, feature_portion)
    send_slots = send_slots.reshape(wide_count, capacity)
    down_matrix = adapter_down_maps.reshape(feature_portion, present_adapters * rank_dimension)
    up_matrix = adapter_up_maps.reshape(present_adapters * rank_dimension, column_portion)
    column_adapter = (
        jnp.arange(present_adapters * rank_dimension, dtype=jnp.int32) // rank_dimension
    )
    got_rows = lax.all_to_all(send_rows, "wide", split_axis=0, concat_axis=0, tiled=True)
    got_slots = lax.all_to_all(send_slots, "wide", split_axis=0, concat_axis=0, tiled=True)
    source_rows, entry_list = got_slots.shape
    flat_rows = got_rows.reshape(source_rows * entry_list, feature_portion)
    slot_adapter = got_slots.reshape(source_rows * entry_list)
    all_ranks = jnp.dot(flat_rows, down_matrix, preferred_element_type=jnp.float32)
    selected = slot_adapter[:, None] == column_adapter[None, :]
    partial_value = jnp.sum(
        jnp.where(selected, all_ranks, 0.0).reshape(
            source_rows * entry_list, present_adapters, rank_dimension
        ),
        axis=1,
    )
    summed = lax.psum(partial_value, "tensor")
    reduced_rows = summed.astype(jnp.bfloat16)
    expanded_rows = jnp.where(
        selected, jnp.tile(reduced_rows, (1, present_adapters)), jnp.zeros((), jnp.bfloat16)
    )
    adapter_correction = jnp.dot(
        expanded_rows, up_matrix, preferred_element_type=jnp.float32
    ).astype(jnp.bfloat16)
    adapter_correction = adapter_correction.reshape(source_rows, entry_list, column_portion)
    returned_rows = lax.all_to_all(
        adapter_correction, "wide", split_axis=0, concat_axis=0, tiled=True
    )
    returned_rows = returned_rows.reshape(wide_count * capacity, column_portion)
    adapter_row_output = returned_rows[storage_slot_index]
    return (base_projection_output + adapter_row_output.astype(jnp.float32)).astype(jnp.bfloat16)


def solution(mesh):
    in_specs = (
        P("wide", "tensor"),
        P(None, "tensor"),
        P("tensor", "wide", None),
        P("wide", None, "tensor"),
        P("wide"),
        P(),
    )
    out_specs = P("wide", "tensor")
    return jax.shard_map(body, mesh=mesh, in_specs=in_specs, out_specs=out_specs, check_vma=False)
```

profile of v0, /device:TPU:24, one launch (start us, length us, event | category | flops | bytes accessed | tf_op | source)
XLA Modules:
  0.0 157.6 jit_solution(14151198750834206589)
XLA Ops:
  6.5 0.7 all-gather.2.cloned.1.call-update
  7.3 0.9 select_reduce_fusion
  8.2 1.2 reduce-window.6
  9.4 0.2 slice_reduce_fusion
  9.7 0.1 fusion.12
  9.8 2.4 %scatter_custom_fusion = s32[1024]{0:T(1024)S(1)} fusion(s32[512]{0:T(512)S(1)} %bitcast.57, s32[512]{0:T(512)S(1)} %get-tuple-element.5, s32[]{:T(128)} %constant.50.clone.1), kind=kCustom, calls=%fused_computation.59 | custom fusion | bytes 4100 | tf_op jit(solution)/shard_map/scatter | solution.py:41
  12.3 0.7 all_to_all.12
  13.0 13.2 %all-to-all-start = ((s32[32,1,32]{2,1,0:T(1,128)}), s32[32,1,32]{2,1,0:T(1,128)S(1)}, u32[]{:S(2)}, u32[]{:S(2)}) async-start(s32[32,1,32]{2,1,0:T(1,128)} %all_to_all.12), calls=%async_computation | async-start | bytes 32768 | tf_op jit(solution)/shard_map/all_to_all | solution.py:51
  26.1 4.1 %scatter_custom_fusion.1 = bf16[1024,512]{1,0:T(8,128)(2,1)} fusion(s32[512]{0:T(512)S(1)} %bitcast.58, bf16[512,512]{1,0:T(8,128)(2,1)} %param.6, bf16[]{:T(256)} %constant.61.clone.1), kind=kCustom, calls=%fused_computation.16 | custom fusion | bytes 1049088 | tf_op jit(solution)/shard_map/scatter | solution.py:38
  30.2 5.6 %all-to-all-done = s32[32,1,32]{2,1,0:T(1,128)S(1)} async-done(((s32[32,1,32]{2,1,0:T(1,128)}), s32[32,1,32]{2,1,0:T(1,128)S(1)}, u32[]{:S(2)}, u32[]{:S(2)}) %all-to-all-start) | async-done | bytes 4128 | tf_op jit(solution)/shard_map/all_to_all | solution.py:51
  35.8 4.2 %all-to-all-start.1 = ((bf16[32,32,512]{2,1,0:T(8,128)(2,1)}), bf16[32,32,512]{2,1,0:T(8,128)(2,1)S(1)}, u32[]{:S(2)}, u32[]{:S(2)}) async-start(bf16[32,32,512]{2,1,0:T(8,128)(2,1)} %bitcast.5), calls=%async_computation.1 | async-start | bytes 2097152 | tf_op jit(solution)/shard_map/all_to_all | solution.py:50
  40.0 0.5 broadcast.228
  40.5 0.7 reduce.5
  41.2 0.1 eq.71
  41.3 26.2 %all-to-all-done.1 = bf16[32,32,512]{2,1,0:T(8,128)(2,1)S(1)} async-done(((bf16[32,32,512]{2,1,0:T(8,128)(2,1)}), bf16[32,32,512]{2,1,0:T(8,128)(2,1)S(1)}, u32[]{:S(2)}, u32[]{:S(2)}) %all-to-all-start.1) | async-done | bytes 1048608 | tf_op jit(solution)/shard_map/all_to_all | solution.py:50
  67.5 4.5 %compare_select_fusion = f32[1024,1024]{0,1:T(8,128)} fusion(bf16[1024,512]{1,0:T(8,128)(2,1)S(1)} %bitcast.55, bf16[512,1024]{0,1:T(8,128)(2,1)} %bitcast.61, s32[1024]{0:T(1024)S(1)} %eq.71, s32[1024]{0:T(1024)S(1)} %add_select_fusion.1), kind=kOutput, calls=%fused_computation.3 | convolution fusion | flops 1075838976 | bytes 6299648 | tf_op jit(solution)/shard_map/dot_general | solution.py:55
  72.0 2.5 %reduce_sum.38 = f32[1024,64]{0,1:T(8,128)S(1)} reduce(f32[1024,16,64]{0,2,1:T(8,128)} %bitcast.54, f32[]{:T(128)} %constant.62.clone.1), dimensions={1}, to_apply=%region_6.7 | reduce | flops 983040 | bytes 4456452 | tf_op jit(solution)/shard_map/reduce_sum | solution.py:57
  74.5 47.2 %all-reduce.1 = bf16[1024,64]{0,1:T(8,128)(2,1)S(1)} all-reduce(f32[1024,64]{0,1:T(8,128)S(1)} %reduce_sum.38), channel_id=1, replica_groups=mesh['wide'=32,'tensor'=16] {'tensor'}, use_global_device_ids=true, to_apply=%region_7.8 | all-reduce | flops 65536 | bytes 393216 | tf_op jit(solution)/shard_map/psum | solution.py:63
  121.7 1.7 %fusion.4 = bf16[1024,128]{1,0:T(8,128)(2,1)} fusion(bf16[16,64,128]{2,1,0:T(8,128)(2,1)S(1)} %copy-done.1, s32[16,64]{1,0:T(8,128)S(1)} %add_select_fusion, s32[1024]{0:T(1024)S(1)} %eq.71, bf16[1024,64]{0,1:T(8,128)(2,1)S(1)} %all-reduce.1), kind=kOutput, calls=%fused_computation.9 | convolution fusion | flops 270663680 | bytes 663552 | tf_op jit(solution)/shard_map/dot_general | solution.py:68
  123.4 5.7 %all-to-all-start.2 = ((bf16[32,32,128]{2,1,0:T(8,128)(2,1)}), bf16[32,32,128]{2,1,0:T(8,128)(2,1)S(1)}, u32[]{:S(2)}, u32[]{:S(2)}) async-start(bf16[32,32,128]{2,1,0:T(8,128)(2,1)} %bitcast.10), calls=%async_computation.2 | async-start | bytes 524288 | tf_op jit(solution)/shard_map/all_to_all | solution.py:72
  129.1 13.9 %all-to-all-done.2 = bf16[32,32,128]{2,1,0:T(8,128)(2,1)S(1)} async-done(((bf16[32,32,128]{2,1,0:T(8,128)(2,1)}), bf16[32,32,128]{2,1,0:T(8,128)(2,1)S(1)}, u32[]{:S(2)}, u32[]{:S(2)}) %all-to-all-start.2) | async-done | bytes 262176 | tf_op jit(solution)/shard_map/all_to_all | solution.py:72
  143.0 1.3 gather_fusion
  144.3 0.0 all-gather.2.cloned.1.call-done
  144.4 6.4 %fusion.5 = bf16[512,128]{1,0:T(8,128)(2,1)} fusion(bf16[512,8192]{1,0:T(8,128)(2,1)} %all-gather.2.cloned.1.call-done, bf16[8192,128]{1,0:T(8,128)(2,1)S(1)} %copy-done, bf16[512,128]{1,0:T(8,128)(2,1)S(1)} %gather_fusion), kind=kOutput, calls=%fused_computation.11 | convolution fusion | flops 1073938432 | bytes 10747904 | tf_op jit(solution)/shard_map/dot_general | solution.py:23
  (14 shorter events, 0.1 us)
Async XLA Ops:
  6.5 137.8 %copy-start = (bf16[8192,128]{1,0:T(8,128)(2,1)S(1)}, bf16[8192,128]{1,0:T(8,128)(2,1)}, u32[]{:S(2)}) copy-start(bf16[8192,128]{1,0:T(8,128)(2,1)} %param.7) | copy-start | bytes 6291460
  6.5 137.8 %all-gather.2.cloned.1.call-start = ((), (), s32[]{:S(2)}) async-start(), calls=%async_computation.3 | async-start | bytes 8912896 | tf_op jit(solution)/shard_map/all_gather | solution.py:22
  13.0 22.8 %all-to-all-start = ((s32[32,1,32]{2,1,0:T(1,128)}), s32[32,1,32]{2,1,0:T(1,128)S(1)}, u32[]{:S(2)}, u32[]{:S(2)}) async-start(s32[32,1,32]{2,1,0:T(1,128)} %all_to_all.12), calls=%async_computation | async-start | bytes 32768 | tf_op jit(solution)/shard_map/all_to_all | solution.py:51
  35.8 31.7 %all-to-all-start.1 = ((bf16[32,32,512]{2,1,0:T(8,128)(2,1)}), bf16[32,32,512]{2,1,0:T(8,128)(2,1)S(1)}, u32[]{:S(2)}, u32[]{:S(2)}) async-start(bf16[32,32,512]{2,1,0:T(8,128)(2,1)} %bitcast.5), calls=%async_computation.1 | async-start | bytes 2097152 | tf_op jit(solution)/shard_map/all_to_all | solution.py:50
  71.9 49.7 %copy-start.1 = (bf16[16,64,128]{2,1,0:T(8,128)(2,1)S(1)}, bf16[16,64,128]{2,1,0:T(8,128)(2,1)}, u32[]{:S(2)}) copy-start(bf16[16,64,128]{2,1,0:T(8,128)(2,1)} %param.9) | copy-start | bytes 786436
  123.4 19.6 %all-to-all-start.2 = ((bf16[32,32,128]{2,1,0:T(8,128)(2,1)}), bf16[32,32,128]{2,1,0:T(8,128)(2,1)S(1)}, u32[]{:S(2)}, u32[]{:S(2)}) async-start(bf16[32,32,128]{2,1,0:T(8,128)(2,1)} %bitcast.10), calls=%async_computation.2 | async-start | bytes 524288 | tf_op jit(solution)/shard_map/all_to_all | solution.py:72
Sparse Core Ops, SparseCore 0:
  9.5 62.3 all-gather.1
where the time goes:
time: 158 us
  blocking collectives  47.2 us (30%)
  waiting for transfers between devices  46.4 us (29%)
  starting transfers between devices  23 us (15%)
  between operations  13.5 us (9%)
  matrix products  12.6 us (8%)
  local copies, waits for them, and re-layouts  9.34 us (6%)
  other arithmetic  5.53 us (4%)
    psum x1, blocking collectives, body(): summed = lax.psum(partial_value, 'tensor')  47.2 us
    all_to_all x1, waiting for transfers between devices, body(): lax.all_to_all(send_rows, 'wide', split_axis=0, concat_axis=0, tiled=True)  26.2 us
    all_to_all x1, waiting for transfers between devices, body(): lax.all_to_all(adapter_correction, 'wide', split_axis=0, concat_axis=0, t...  13.9 us
    all_to_all x1, starting transfers between devices, body(): lax.all_to_all(send_slots, 'wide', split_axis=0, concat_axis=0, tiled=True)  13.2 us
    dot_general x1, matrix products, body(): jnp.dot(gathered, key_value_weight, preferred_element_type=jnp.float32)  6.39 us
    all_to_all x1, starting transfers between devices, body(): lax.all_to_all(adapter_correction, 'wide', split_axis=0, concat_axis=0, t...  5.67 us
    all_to_all x1, waiting for transfers between devices, body(): lax.all_to_all(send_slots, 'wide', split_axis=0, concat_axis=0, tiled=True)  5.61 us
    dot_general x1, matrix products, body(): jnp.dot(flat_rows, down_matrix, preferred_element_type=jnp.float32)  4.49 us
  transfers between devices with their start and end apart: 4, of which 3 were waited for; matrix products, arithmetic and copies ran while one was open for 13% of the time, Pallas kernels for 0%

commit v1 on v0

--- a/solution.py
+++ b/solution.py
@@ -60,7 +60,7 @@
         ),
         axis=1,
     )
-    summed = lax.psum(partial_value, "tensor")
+    summed = jnp.sum(lax.all_gather(partial_value, "tensor"), axis=0)
     reduced_rows = summed.astype(jnp.bfloat16)
     expanded_rows = jnp.where(
         selected, jnp.tile(reduced_rows, (1, present_adapters)), jnp.zeros((), jnp.bfloat16)

time: 158 us -> 191 us (1.21)
  the two profiles are of different devices: /device:TPU:24 before, /device:TPU:1 now
where the time goes in v1:
time: 191 us; the launch traced here: 190 us
  waiting for transfers between devices  115 us (60%)
  starting transfers between devices  28.6 us (15%)
  local copies, waits for them, and re-layouts  13.9 us (7%)
  between operations  13.5 us (7%)
  matrix products  12.5 us (7%)
  other arithmetic  7.17 us (4%)
    all_gather x1, waiting for transfers between devices, body(): summed = jnp.sum(lax.all_gather(partial_value, 'tensor'), axis=0)  44.2 us
    all_gather x1, waiting for transfers between devices, body(): gathered = lax.all_gather(tokens, 'tensor', axis=1, tiled=True)  29.4 us
    all_to_all x1, waiting for transfers between devices, body(): lax.all_to_all(send_rows, 'wide', split_axis=0, concat_axis=0, tiled=True)  24.3 us
    all_to_all x1, starting transfers between devices, body(): lax.all_to_all(send_slots, 'wide', split_axis=0, concat_axis=0, tiled=True)  13.7 us
    all_to_all x1, waiting for transfers between devices, body(): lax.all_to_all(adapter_correction, 'wide', split_axis=0, concat_axis=0, t...  11.5 us
    all_to_all x1, starting transfers between devices, body(): lax.all_to_all(adapter_correction, 'wide', split_axis=0, concat_axis=0, t...  10.1 us
    dot_general x1, matrix products, body(): jnp.dot(gathered, key_value_weight, preferred_element_type=jnp.float32)  6.39 us
    all_to_all x1, starting transfers between devices, body(): lax.all_to_all(send_rows, 'wide', split_axis=0, concat_axis=0, tiled=True)  4.68 us
  transfers between devices with their start and end apart: 5, of which 5 were waited for; matrix products, arithmetic and copies ran while one was open for 7% of the time, Pallas kernels for 0%

profile of v1, /device:TPU:1, one launch (start us, length us, event | category | flops | bytes accessed | tf_op | source)
XLA Modules:
  0.0 190.4 jit_solution(4802829308427890857)
XLA Ops:
  6.5 1.1 select_reduce_fusion
  7.7 1.2 reduce-window.6
  8.8 0.2 slice_reduce_fusion
  9.2 2.4 %scatter_custom_fusion = s32[1024]{0:T(1024)S(1)} fusion(s32[512]{0:T(512)S(1)} %bitcast.63, s32[512]{0:T(512)S(1)} %get-tuple-element.5, s32[]{:T(128)} %constant.50.clone.1), kind=kCustom, calls=%fused_computation.60 | custom fusion | bytes 4100 | tf_op jit(solution)/shard_map/scatter | solution.py:41
  11.7 0.7 all_to_all.12
  12.4 13.7 %all-to-all-start = ((s32[32,1,32]{2,1,0:T(1,128)}), s32[32,1,32]{2,1,0:T(1,128)S(1)}, u32[]{:S(2)}, u32[]{:S(2)}) async-start(s32[32,1,32]{2,1,0:T(1,128)} %all_to_all.12), calls=%async_computation | async-start | bytes 32768 | tf_op jit(solution)/shard_map/all_to_all | solution.py:51
  26.1 4.0 %scatter_custom_fusion.1 = bf16[1024,512]{1,0:T(8,128)(2,1)} fusion(s32[512]{0:T(512)S(1)} %bitcast.64, bf16[512,512]{1,0:T(8,128)(2,1)} %param.6, bf16[]{:T(256)} %constant.61.clone.1), kind=kCustom, calls=%fused_computation.17 | custom fusion | bytes 1049088 | tf_op jit(solution)/shard_map/scatter | solution.py:38
  30.1 4.5 %all-to-all-done = s32[32,1,32]{2,1,0:T(1,128)S(1)} async-done(((s32[32,1,32]{2,1,0:T(1,128)}), s32[32,1,32]{2,1,0:T(1,128)S(1)}, u32[]{:S(2)}, u32[]{:S(2)}) %all-to-all-start) | async-done | bytes 4128 | tf_op jit(solution)/shard_map/all_to_all | solution.py:51
  34.6 4.7 %all-to-all-start.1 = ((bf16[32,32,512]{2,1,0:T(8,128)(2,1)}), bf16[32,32,512]{2,1,0:T(8,128)(2,1)S(1)}, u32[]{:S(2)}, u32[]{:S(2)}) async-start(bf16[32,32,512]{2,1,0:T(8,128)(2,1)} %bitcast.5), calls=%async_computation.1 | async-start | bytes 2097152 | tf_op jit(solution)/shard_map/all_to_all | solution.py:50
  39.4 0.5 broadcast.228
  39.9 0.7 reduce.5
  40.7 24.3 %all-to-all-done.1 = bf16[32,32,512]{2,1,0:T(8,128)(2,1)S(1)} async-done(((bf16[32,32,512]{2,1,0:T(8,128)(2,1)}), bf16[32,32,512]{2,1,0:T(8,128)(2,1)S(1)}, u32[]{:S(2)}, u32[]{:S(2)}) %all-to-all-start.1) | async-done | bytes 1048608 | tf_op jit(solution)/shard_map/all_to_all | solution.py:50
  65.0 4.4 %compare_select_fusion = f32[1024,1024]{0,1:T(8,128)} fusion(bf16[1024,512]{1,0:T(8,128)(2,1)S(1)} %bitcast.61, bf16[512,1024]{0,1:T(8,128)(2,1)} %bitcast.67, s32[1024]{0:T(1024)S(1)} %eq.71, s32[1024]{0:T(1024)S(1)} %add_select_fusion.1), kind=kOutput, calls=%fused_computation.4 | convolution fusion | flops 1075838976 | bytes 6299648 | tf_op jit(solution)/shard_map/dot_general | solution.py:55
  69.4 3.2 %reduce_sum.47 = f32[1024,64]{0,1:T(8,128)} reduce(f32[1024,16,64]{0,2,1:T(8,128)} %bitcast.59, f32[]{:T(128)} %constant.62.clone.1), dimensions={1}, to_apply=%region_6.7 | reduce | flops 983040 | bytes 4456452 | tf_op jit(solution)/shard_map/reduce_sum | solution.py:57
  72.7 0.7 all-gather.4.cloned.1.call-update
  73.4 44.2 %all-gather.6.cloned.1.call-done = f32[16384,64]{0,1:T(8,128)} async-done(((f32[1024,64]{0,1:T(8,128)}), f32[16384,64]{0,1:T(8,128)}) %all-gather.6.cloned.1.call-update) | async-done | bytes 4194320 | tf_op jit(solution)/shard_map/all_gather | solution.py:63
  117.6 4.6 %copy.11 = f32[8,8,16,1024]{3,2,1,0:T(8,128)S(1)} copy(f32[8,8,16,1024]{3,1,2,0:T(8,128)} %bitcast.60) | data formatting | bytes 8388608
  122.1 0.8 bitcast_reduce_fusion
  123.1 1.7 fusion.4
  124.8 10.1 %all-to-all-start.2 = ((bf16[32,32,128]{2,1,0:T(8,128)(2,1)}), bf16[32,32,128]{2,1,0:T(8,128)(2,1)S(1)}, u32[]{:S(2)}, u32[]{:S(2)}) async-start(bf16[32,32,128]{2,1,0:T(8,128)(2,1)} %bitcast.10), calls=%async_computation.2 | async-start | bytes 524288 | tf_op jit(solution)/shard_map/all_to_all | solution.py:72
  134.9 11.5 %all-to-all-done.2 = bf16[32,32,128]{2,1,0:T(8,128)(2,1)S(1)} async-done(((bf16[32,32,128]{2,1,0:T(8,128)(2,1)}), bf16[32,32,128]{2,1,0:T(8,128)(2,1)S(1)}, u32[]{:S(2)}, u32[]{:S(2)}) %all-to-all-start.2) | async-done | bytes 262176 | tf_op jit(solution)/shard_map/all_to_all | solution.py:72
  146.4 1.3 gather_fusion
  147.7 29.4 %all-gather.4.cloned.1.call-done = bf16[512,8192]{1,0:T(8,128)(2,1)} async-done(((bf16[512,512]{1,0:T(8,128)(2,1)}), bf16[512,8192]{1,0:T(8,128)(2,1)}) %all-gather.4.cloned.1.call-update) | async-done | bytes 8388624 | tf_op jit(solution)/shard_map/all_gather | solution.py:22
  177.1 6.4 %fusion.5 = bf16[512,128]{1,0:T(8,128)(2,1)} fusion(bf16[512,8192]{1,0:T(8,128)(2,1)} %all-gather.4.cloned.1.call-done, bf16[8192,128]{1,0:T(8,128)(2,1)S(1)} %copy-done, bf16[512,128]{1,0:T(8,128)(2,1)S(1)} %gather_fusion), kind=kOutput, calls=%fused_computation.12 | convolution fusion | flops 1073938432 | bytes 10747904 | tf_op jit(solution)/shard_map/dot_general | solution.py:23
  (18 shorter events, 0.5 us)
Async XLA Ops:
  6.5 170.6 %copy-start = (bf16[8192,128]{1,0:T(8,128)(2,1)S(1)}, bf16[8192,128]{1,0:T(8,128)(2,1)}, u32[]{:S(2)}) copy-start(bf16[8192,128]{1,0:T(8,128)(2,1)} %param.7) | copy-start | bytes 6291460
  12.4 22.2 %all-to-all-start = ((s32[32,1,32]{2,1,0:T(1,128)}), s32[32,1,32]{2,1,0:T(1,128)S(1)}, u32[]{:S(2)}, u32[]{:S(2)}) async-start(s32[32,1,32]{2,1,0:T(1,128)} %all_to_all.12), calls=%async_computation | async-start | bytes 32768 | tf_op jit(solution)/shard_map/all_to_all | solution.py:51
  34.6 30.4 %all-to-all-start.1 = ((bf16[32,32,512]{2,1,0:T(8,128)(2,1)}), bf16[32,32,512]{2,1,0:T(8,128)(2,1)S(1)}, u32[]{:S(2)}, u32[]{:S(2)}) async-start(bf16[32,32,512]{2,1,0:T(8,128)(2,1)} %bitcast.5), calls=%async_computation.1 | async-start | bytes 2097152 | tf_op jit(solution)/shard_map/all_to_all | solution.py:50
  39.3 78.2 %all-gather.6.cloned.1.call-start = ((), (), s32[]{:S(2)}) async-start(), calls=%async_computation.4 | async-start | bytes 4456448 | tf_op jit(solution)/shard_map/all_gather | solution.py:63
  72.6 104.5 %all-gather.4.cloned.1.call-start = ((), (), s32[]{:S(2)}) async-start(), calls=%async_computation.3 | async-start | bytes 8912896 | tf_op jit(solution)/shard_map/all_gather | solution.py:22
  122.1 1.0 copy-start.1
  124.8 21.6 %all-to-all-start.2 = ((bf16[32,32,128]{2,1,0:T(8,128)(2,1)}), bf16[32,32,128]{2,1,0:T(8,128)(2,1)S(1)}, u32[]{:S(2)}, u32[]{:S(2)}) async-start(bf16[32,32,128]{2,1,0:T(8,128)(2,1)} %bitcast.10), calls=%async_computation.2 | async-start | bytes 524288 | tf_op jit(solution)/shard_map/all_to_all | solution.py:72
Sparse Core Ops, SparseCore 0:
  72.8 44.7 all-gather.5
  119.7 57.3 all-gather.3
